TPU v7x, 128 devices: a whole 4x4x4 slice. The times are simulated.
128 devices in a mesh: rep: 4 (over z), shard: 32 (over x, y, core).
Axes of the slice: x: 4, y: 4, z: 4, core: 2. Of those that a mesh axis runs over, the one named last changes fastest.
Arguments:
- trained_sq: float32 [4, 4, 768, 768], P('rep', None, 'shard'), may hold values from -6 to 6
- trained_up: float32 [4, 768, 3072], P('rep', 'shard'), may hold values from -6 to 6
- trained_down: float32 [4, 3072, 768], P('rep', 'shard'), may hold values from -6 to 6
- trained_ln: float32 [4, 4, 768], P('rep', None, 'shard'), may hold values from -6 to 6
- start_sq: float32 [4, 768, 768], P(None, 'shard'), may hold values from -6 to 6
- start_up: float32 [768, 3072], P('shard'), may hold values from -6 to 6
- start_down: float32 [3072, 768], P('shard'), may hold values from -6 to 6
- start_ln: float32 [4, 768], P(None, 'shard'), may hold values from -6 to 6
- resid_sq: float32 [4, 4, 768, 768], P('rep', None, 'shard'), may hold values from -4 to 4
- resid_up: float32 [4, 768, 3072], P('rep', 'shard'), may hold values from -4 to 4
- resid_down: float32 [4, 3072, 768], P('rep', 'shard'), may hold values from -4 to 4
- mom_sq: float32 [4, 768, 768], P(None, 'shard'), may hold values from -3 to 3
- mom_up: float32 [768, 3072], P('shard'), may hold values from -3 to 3
- mom_down: float32 [3072, 768], P('shard'), may hold values from -3 to 3
- mom_ln: float32 [4, 768], P(None, 'shard'), may hold values from -3 to 3
- basis_sq: float32 [4, 768, 64], replicated, may hold values from -0.21875 to 0.21875
- basis_up: float32 [3072, 64], replicated, may hold values from -0.109375 to 0.109375
- basis_down: float32 [768, 64], replicated, may hold values from -0.21875 to 0.21875
Outputs:
- new_resid_sq: float32 [4, 4, 768, 768], P('rep', None, 'shard')
- new_resid_up: float32 [4, 768, 3072], P('rep', 'shard')
- new_resid_down: float32 [4, 3072, 768], P('rep', 'shard')
- new_mom_sq: float32 [4, 768, 768], P(None, 'shard')
- new_mom_up: float32 [768, 3072], P('shard')
- new_mom_down: float32 [3072, 768], P('shard')
- new_mom_ln: float32 [4, 768], P(None, 'shard')
- weights_sq: bfloat16 [4, 768, 768], replicated
- weights_up: bfloat16 [768, 3072], replicated
- weights_down: bfloat16 [3072, 768], replicated
- weights_ln: bfloat16 [4, 768], replicated
All inputs are finite; a program needn't handle non-finite values.
Results may differ from a plain program's by a relative error of at most 0.001.
Values may be sent and summed in bfloat16 or wider, within the bound.
No kernel may reach another device: no remote copies, remote signals or barrier semaphores. Data moves between devices by JAX's collectives and lax.ppermute only.
A program may use at most 128 MiB of HBM per device.

v0:
```python
import jax
import jax.numpy as jnp
from jax import lax
from jax.sharding import PartitionSpec as P

moment_coef = 0.9
outer_rate = 0.7


def advance(start, moment, outer):
    new_moment = moment_coef * moment + outer
    weights = (start - outer_rate * (outer + moment_coef * new_moment)).astype(jnp.bfloat16)
    return (new_moment, weights)


def on_device(
    trained_sq,
    trained_up,
    trained_down,
    trained_ln,
    start_sq,
    start_up,
    start_down,
    start_ln,
    resid_sq,
    resid_up,
    resid_down,
    mom_sq,
    mom_up,
    mom_down,
    mom_ln,
    basis_sq,
    basis_up,
    basis_down,
):
    highest = lax.Precision.HIGHEST
    groups = lax.axis_size("rep")
    delta_sq = start_sq - trained_sq[0] + resid_sq[0]
    factor_sq = jnp.einsum("mrd,mdk->mrk", delta_sq, basis_sq, precision=highest)
    new_resid_sq = delta_sq - jnp.einsum("mrk,mdk->mrd", factor_sq, basis_sq, precision=highest)
    delta_up = start_up - trained_up[0] + resid_up[0]
    factor_up = jnp.dot(delta_up, basis_up, precision=highest, preferred_element_type=jnp.float32)
    new_resid_up = delta_up - jnp.einsum("rk,fk->rf", factor_up, basis_up, precision=highest)
    delta_down = start_down - trained_down[0] + resid_down[0]
    factor_down = jnp.dot(
        delta_down, basis_down, precision=highest, preferred_element_type=jnp.float32
    )
    new_resid_down = delta_down - jnp.einsum(
        "rk,dk->rd", factor_down, basis_down, precision=highest
    )
    norm_delta = start_ln - trained_ln[0]
    summed = lax.psum((factor_sq, factor_up, factor_down, norm_delta), "rep")
    mean_sq = summed[0] / groups
    mean_up = summed[1] / groups
    mean_down = summed[2] / groups
    mean_ln = summed[3] / groups
    new_mom_ln, norm_weights = advance(start_ln, mom_ln, mean_ln)
    outer_sq = jnp.einsum("mrk,mdk->mrd", mean_sq, basis_sq, precision=highest)
    outer_up = jnp.einsum("rk,fk->rf", mean_up, basis_up, precision=highest)
    outer_down = jnp.einsum("rk,dk->rd", mean_down, basis_down, precision=highest)
    new_mom_sq, owned_sq = advance(start_sq, mom_sq, outer_sq)
    new_mom_up, owned_up = advance(start_up, mom_up, outer_up)
    new_mom_down, owned_down = advance(start_down, mom_down, outer_down)
    weights_sq, weights_up, weights_down, weights_ln = (
        lax.all_gather(owned_sq, "shard", axis=1, tiled=True),
        lax.all_gather(owned_up, "shard", axis=0, tiled=True),
        lax.all_gather(owned_down, "shard", axis=0, tiled=True),
        lax.all_gather(norm_weights, "shard", axis=1, tiled=True),
    )
    return (
        new_resid_sq[None],
        new_resid_up[None],
        new_resid_down[None],
        new_mom_sq,
        new_mom_up,
        new_mom_down,
        new_mom_ln,
        weights_sq,
        weights_up,
        weights_down,
        weights_ln,
    )


def solution(mesh):
    placed = (
        P("rep", None, "shard", None),
        P("rep", "shard", None),
        P("rep", "shard", None),
        P("rep", None, "shard"),
        P(None, "shard", None),
        P("shard", None),
        P("shard", None),
        P(None, "shard"),
        P("rep", None, "shard", None),
        P("rep", "shard", None),
        P("rep", "shard", None),
        P(None, "shard", None),
        P("shard", None),
        P("shard", None),
        P(None, "shard"),
        P(),
        P(),
        P(),
    )
    return jax.shard_map(
        on_device,
        mesh=mesh,
        in_specs=placed,
        out_specs=(
            P("rep", None, "shard", None),
            P("rep", "shard", None),
            P("rep", "shard", None),
            P(None, "shard", None),
            P("shard", None),
            P("shard", None),
            P(None, "shard"),
            P(),
            P(),
            P(),
            P(),
        ),
        check_vma=False,
    )
```

profile of v0, /device:TPU:1, one launch (start us, length us, event | category | flops | bytes accessed | tf_op | source)
XLA Modules:
  0.0 201.4 jit_solution(2891028444277751555)
XLA Ops:
  7.2 0.0 copy-start
  7.2 0.0 copy-start.5
  7.2 0.0 copy-start.4
  7.2 0.0 copy-start.6
  7.2 0.0 copy-start.3
  7.2 0.0 copy-start.1
  7.3 0.0 all-gather.5.cloned.1.call-start
  7.3 0.9 bitcast_subtract_fusion.3
  8.2 0.5 copy-done
  8.7 0.0 copy-start.9
  8.7 2.6 %fusion.16 = f32[4,24,64]{2,1,0:T(8,128)} fusion(f32[4,768,64]{1,2,0:T(8,128)S(1)} %copy-done, f32[1,4,24,768]{3,2,1,0:T(8,128)} %param.26, f32[4,24,768]{2,1,0:T(8,128)} %param.22, f32[1,4,24,768]{3,2,1,0:T(8,128)} %param.18), kind=kOutput, calls=%fused_computation.34 | convolution fusion | flops 56770560 | bytes 1695744 | tf_op jit(solution)/shard_map/mrd,mdk->mrk/dot_general | solution.py:39
  11.2 0.0 copy-start.7
  11.2 2.3 %fusion.18 = f32[96,64]{0,1:T(8,128)} fusion(f32[768,64]{0,1:T(8,128)} %param.35, f32[1,96,768]{2,1,0:T(8,128)} %param.28, f32[96,768]{1,0:T(8,128)} %param.24, f32[1,96,768]{2,1,0:T(8,128)} %param.20), kind=kOutput, calls=%fused_computation.36 | convolution fusion | flops 56770560 | bytes 1105920 | tf_op jit(solution)/shard_map/dot_general | solution.py:45
  13.5 2.1 %fusion.17 = f32[24,64]{1,0:T(8,128)S(1)} fusion(f32[3072,64]{0,1:T(8,128)} %param.34, f32[1,24,3072]{2,1,0:T(8,128)} %param.27, f32[24,3072]{1,0:T(8,128)} %param.23, f32[1,24,3072]{2,1,0:T(8,128)} %param.19), kind=kOutput, calls=%fused_computation.35 | convolution fusion | flops 56770560 | bytes 1677312 | tf_op jit(solution)/shard_map/dot_general | solution.py:42
  15.6 17.3 %all-reduce = (f32[4,24,64]{2,1,0:T(8,128)}, f32[24,64]{1,0:T(8,128)}, f32[96,64]{0,1:T(8,128)}, f32[4,24]{1,0:T(4,128)}) all-reduce(f32[4,24,64]{2,1,0:T(8,128)} %fusion.16, f32[24,64]{1,0:T(8,128)S(1)} %fusion.17, f32[96,64]{0,1:T(8,128)} %fusion.18, f32[4,24]{1,0:T(4,128)S(1)} %bitcast_subtract_fusion.3), channel_id=1, replica_groups=mesh['rep'=4,'shard'=32] {'rep'}, use_global_device_ids=true, to_apply=%region_0.0 | all-reduce | flops 13920 | bytes 111360 | tf_op jit(solution)/shard_map/psum | solution.py:52
  33.0 0.0 copy-done.5
  33.0 2.3 %subtract_convert_fusion.2 = (bf16[4,24,768]{2,1,0:T(8,128)(2,1)}, f32[4,24,768]{2,1,0:T(8,128)}) fusion(f32[4,24,768]{2,1,0:T(8,128)S(1)} %copy-done.5, f32[4,24,768]{2,1,0:T(8,128)} %param.29, f32[4,768,64]{1,2,0:T(8,128)S(1)} %copy-done, f32[4,24,64]{2,1,0:T(8,128)} %get-tuple-element.11), kind=kOutput, calls=%fused_computation.14 | convolution fusion | flops 57145344 | bytes 1843200 | tf_op jit(solution)/shard_map/mrk,mdk->mrd/dot_general | solution.py:58
  35.3 0.0 all-gather.5.cloned.1.call-update
  35.3 0.0 all-gather.7.cloned.1.call-start
  35.3 0.0 copy-done.3
  35.3 0.0 copy-done.1
  35.4 2.3 %subtract_convert_fusion.1 = (bf16[24,3072]{1,0:T(8,128)(2,1)}, f32[24,3072]{1,0:T(8,128)}) fusion(f32[24,3072]{1,0:T(8,128)S(1)} %copy-done.3, f32[24,3072]{1,0:T(8,128)} %param.30, f32[3072,64]{0,1:T(8,128)S(1)} %copy-done.1, f32[24,64]{1,0:T(8,128)} %get-tuple-element.12), kind=kOutput, calls=%fused_computation.13 | convolution fusion | flops 57140736 | bytes 1824768 | tf_op jit(solution)/shard_map/rk,fk->rf/dot_general | solution.py:59
  37.6 0.0 all-gather.7.cloned.1.call-update
  37.6 0.0 all-gather.9.cloned.1.call-start
  37.7 0.0 copy-done.4
  37.7 0.0 copy-done.6
  37.7 2.2 %subtract_convert_fusion = (bf16[96,768]{1,0:T(8,128)(2,1)}, f32[96,768]{1,0:T(8,128)}) fusion(f32[96,768]{1,0:T(8,128)S(1)} %copy-done.4, f32[96,768]{1,0:T(8,128)} %param.31, f32[768,64]{0,1:T(8,128)S(1)} %copy-done.6, f32[96,64]{0,1:T(8,128)} %get-tuple-element.13), kind=kOutput, calls=%fused_computation.12 | convolution fusion | flops 57145344 | bytes 1253376 | tf_op jit(solution)/shard_map/rk,dk->rd/dot_general | solution.py:60
  39.9 0.0 all-gather.9.cloned.1.call-update
  40.0 0.0 copy-done.10
  40.0 1.3 fusion.12
  41.3 28.7 %all-gather = bf16[32,24,4]{1,2,0:T(4,128)(2,1)S(1)} all-gather(bf16[1,24,4]{1,2,0:T(4,128)(2,1)S(1)} %get-tuple-element.15), channel_id=1, replica_groups=mesh['rep'=4,'shard'=32] {'shard'}, dimensions={0}, use_global_device_ids=true | all-gather | bytes 6336 | tf_op jit(solution)/shard_map/all_gather | solution.py:68
  69.9 0.6 copy.30
  70.6 1.5 reshape.23
  72.0 0.0 copy-done.9
  72.0 2.1 %fusion.1 = f32[1,96,768]{2,1,0:T(8,128)} fusion(f32[96,64]{0,1:T(8,128)} %fusion.18, f32[768,64]{0,1:T(8,128)S(1)} %copy-done.6, f32[1,96,768]{2,1,0:T(8,128)S(1)} %copy-done.9, f32[96,768]{1,0:T(8,128)S(1)} %copy-done.4, f32[1,96,768]{2,1,0:T(8,128)} %param.20), kind=kOutput, calls=%fused_computation.3 | convolution fusion | flops 56844288 | bytes 1400832 | tf_op jit(solution)/shard_map/rk,dk->rd/dot_general | solution.py:48
  74.2 0.0 copy-done.7
  74.2 0.0 copy-done.8
  74.2 1.2 fusion
  75.4 2.3 %fusion.2 = f32[1,4,24,768]{3,2,1,0:T(8,128)} fusion(f32[4,24,64]{2,1,0:T(8,128)} %fusion.16, f32[4,768,64]{1,2,0:T(8,128)S(1)} %copy-done, f32[1,4,24,768]{3,2,1,0:T(8,128)} %param.26, f32[4,24,768]{2,1,0:T(8,128)S(1)} %copy-done.5, f32[1,4,24,768]{3,2,1,0:T(8,128)} %param.18), kind=kOutput, calls=%fused_computation.5 | convolution fusion | flops 56844288 | bytes 1990656 | tf_op jit(solution)/shard_map/mrk,mdk->mrd/dot_general | solution.py:40
  77.7 8.5 %all-gather.5.cloned.1.call-done = bf16[4,768,768]{2,1,0:T(8,128)(2,1)} async-done(((bf16[4,24,768]{2,1,0:T(8,128)(2,1)}), bf16[4,768,768]{2,1,0:T(8,128)(2,1)}) %all-gather.5.cloned.1.call-update) | async-done | bytes 4718608 | tf_op jit(solution)/shard_map/all_gather | solution.py:65
  86.2 49.0 %all-gather.7.cloned.1.call-done = bf16[768,3072]{1,0:T(8,128)(2,1)} async-done(((bf16[24,3072]{1,0:T(8,128)(2,1)}), bf16[768,3072]{1,0:T(8,128)(2,1)}) %all-gather.7.cloned.1.call-update) | async-done | bytes 4718608 | tf_op jit(solution)/shard_map/all_gather | solution.py:66
  135.1 49.0 %all-gather.9.cloned.1.call-done = bf16[3072,768]{1,0:T(8,128)(2,1)} async-done(((bf16[96,768]{1,0:T(8,128)(2,1)}), bf16[3072,768]{1,0:T(8,128)(2,1)}) %all-gather.9.cloned.1.call-update) | async-done | bytes 4718608 | tf_op jit(solution)/shard_map/all_gather | solution.py:67
  184.1 5.2 %copy.34 = bf16[4,768,768]{2,1,0:T(8,128)(2,1)} copy(bf16[4,768,768]{2,1,0:T(8,128)(2,1)} %all-gather.5.cloned.1.call-done) | data formatting | bytes 9437184
  189.3 0.0 copy-done.2
  189.3 2.4 %copy.35 = bf16[768,3072]{1,0:T(8,128)(2,1)} copy(bf16[768,3072]{1,0:T(8,128)(2,1)S(1)} %copy-done.2) | data formatting | bytes 9437184
  191.7 0.5 slice-done
  192.2 0.5 slice-done.1
  192.7 2.2 %copy.36 = bf16[3072,768]{1,0:T(8,128)(2,1)} copy(bf16[3072,768]{1,0:T(8,128)(2,1)S(1)} %bitcast.64) | data formatting | bytes 9437184
  (6 shorter events, 0.0 us)
Async XLA Ops:
  7.2 1.5 copy-start
  7.2 25.8 %copy-start.5 = (f32[4,24,768]{2,1,0:T(8,128)S(1)}, f32[4,24,768]{2,1,0:T(8,128)}, u32[]{:S(2)}) copy-start(f32[4,24,768]{2,1,0:T(8,128)} %param.22) | copy-start | bytes 884740
  7.2 30.5 %copy-start.4 = (f32[96,768]{1,0:T(8,128)S(1)}, f32[96,768]{1,0:T(8,128)}, u32[]{:S(2)}) copy-start(f32[96,768]{1,0:T(8,128)} %param.24) | copy-start | bytes 884740
  7.2 30.5 %copy-start.6 = (f32[768,64]{0,1:T(8,128)S(1)}, f32[768,64]{0,1:T(8,128)}, u32[]{:S(2)}) copy-start(f32[768,64]{0,1:T(8,128)} %param.35) | copy-start | bytes 589828
  7.2 28.1 %copy-start.3 = (f32[24,3072]{1,0:T(8,128)S(1)}, f32[24,3072]{1,0:T(8,128)}, u32[]{:S(2)}) copy-start(f32[24,3072]{1,0:T(8,128)} %param.23) | copy-start | bytes 884740
  7.2 28.1 %copy-start.1 = (f32[3072,64]{0,1:T(8,128)S(1)}, f32[3072,64]{0,1:T(8,128)}, u32[]{:S(2)}) copy-start(f32[3072,64]{0,1:T(8,128)} %param.34) | copy-start | bytes 2359300
  7.3 78.9 %all-gather.5.cloned.1.call-start = ((), (), s32[]{:S(2)}) async-start(), calls=%async_computation | async-start | bytes 4866048 | tf_op jit(solution)/shard_map/all_gather | solution.py:65
  8.7 63.3 %copy-start.9 = (f32[1,96,768]{2,1,0:T(8,128)S(1)}, f32[1,96,768]{2,1,0:T(8,128)}, u32[]{:S(2)}) copy-start(f32[1,96,768]{2,1,0:T(8,128)} %param.28) | copy-start | bytes 884740
  11.2 62.9 %copy-start.7 = (f32[1,24,3072]{2,1,0:T(8,128)S(1)}, f32[1,24,3072]{2,1,0:T(8,128)}, u32[]{:S(2)}) copy-start(f32[1,24,3072]{2,1,0:T(8,128)} %param.27) | copy-start | bytes 884740
  11.2 62.9 %copy-start.8 = (f32[1,24,3072]{2,1,0:T(8,128)S(1)}, f32[1,24,3072]{2,1,0:T(8,128)}, u32[]{:S(2)}) copy-start(f32[1,24,3072]{2,1,0:T(8,128)} %param.19) | copy-start | bytes 884740
  33.0 7.0 %copy-start.10 = (f32[4,24]{1,0:T(4,128)S(1)}, f32[4,24]{1,0:T(4,128)}, u32[]{:S(2)}) copy-start(f32[4,24]{1,0:T(4,128)} %get-tuple-element.14) | copy-start | bytes 1156
  35.3 99.8 %all-gather.7.cloned.1.call-start = ((), (), s32[]{:S(2)}) async-start(), calls=%async_computation.1 | async-start | bytes 4866048 | tf_op jit(solution)/shard_map/all_gather | solution.py:66
  37.6 146.5 %all-gather.9.cloned.1.call-start = ((), (), s32[]{:S(2)}) async-start(), calls=%async_computation.2 | async-start | bytes 4866048 | tf_op jit(solution)/shard_map/all_gather | solution.py:67
  184.1 5.2 %copy-start.2 = (bf16[768,3072]{1,0:T(8,128)(2,1)S(1)}, bf16[768,3072]{1,0:T(8,128)(2,1)}, u32[]{:S(2)}) copy-start(bf16[768,3072]{1,0:T(8,128)(2,1)} %all-gather.7.cloned.1.call-done) | copy-start | bytes 14155780
  184.1 8.0 %slice-start = ((s8[4718592]{0:T(1024)(128)(4,1)}), s8[4194304]{0:T(1024)(128)(4,1)S(1)}, s32[]{:S(2)}) async-start(s8[4718592]{0:T(1024)(128)(4,1)} %bitcast.63), calls=%async_computation.3 | async-start | bytes 8388608
  189.3 3.4 %slice-start.1 = ((s8[4718592]{0:T(1024)(128)(4,1)}), s8[524288]{0:T(1024)(128)(4,1)S(1)}, s32[]{:S(2)}) async-start(s8[4718592]{0:T(1024)(128)(4,1)} %bitcast.63), calls=%async_computation.4 | async-start | bytes 1048576
Sparse Core Ops, SparseCore 0:
  35.4 50.7 all-gather.4
  89.0 46.0 all-gather.6
  137.9 46.1 all-gather.8
where the time goes:
time: 202 us; the launch traced here: 201 us
  waiting for transfers between devices  106 us (52%)
  blocking collectives  46 us (23%)
  matrix products  19.4 us (10%)
  between operations  13.9 us (7%)
  local copies, waits for them, and re-layouts  13.4 us (7%)
  other arithmetic  2.13 us (1%)
    all_gather x1, waiting for transfers between devices, on_device(): lax.all_gather(owned_down, 'shard', axis=0, tiled=True)  49 us
    all_gather x1, waiting for transfers between devices, on_device(): lax.all_gather(owned_up, 'shard', axis=0, tiled=True)  49 us
    all_gather x1, blocking collectives, on_device(): lax.all_gather(norm_weights, 'shard', axis=1, tiled=True)  28.7 us
    psum x1, blocking collectives, on_device(): summed = lax.psum((factor_sq, factor_up, factor_down, norm_delta), 'rep')  17.3 us
    unnamed x30, local copies, waits for them, and re-layouts  12.8 us
    all_gather x1, waiting for transfers between devices, on_device(): lax.all_gather(owned_sq, 'shard', axis=1, tiled=True)  8.47 us
  transfers between devices with their start and end apart: 3, of which 3 were waited for; matrix products, arithmetic and copies ran while one was open for 7% of the time, Pallas kernels for 0%

commit v1 on v0

--- a/solution.py
+++ b/solution.py
@@ -1,3 +1,4 @@
+import functools
 import jax
 import jax.numpy as jnp
 from jax import lax
@@ -5,6 +6,17 @@
 
 moment_coef = 0.9
 outer_rate = 0.7
+
+
+def _solve_cube(m, array_axis):
+    parts_out = jnp.concatenate(
+        lax.all_to_all(jnp.stack([m for _ in range(lax.axis_size("shard"))]), "shard", 0, 0),
+        axis=array_axis,
+    )
+    return parts_out
+
+
+array_see = functools.partial(_solve_cube, array_axis=0)
 
 
 def advance(start, moment, outer):
@@ -64,7 +76,7 @@
     weights_sq, weights_up, weights_down, weights_ln = (
         lax.all_gather(owned_sq, "shard", axis=1, tiled=True),
         lax.all_gather(owned_up, "shard", axis=0, tiled=True),
-        lax.all_gather(owned_down, "shard", axis=0, tiled=True),
+        array_see(owned_down),
         lax.all_gather(norm_weights, "shard", axis=1, tiled=True),
     )
     return (

time: 202 us -> 190 us (0.941)
  waiting for transfers between devices: 106 us -> 28 us
  blocking collectives: 46 us -> 99.7 us
  starting transfers between devices: 0.12 us -> 11.8 us
  local copies, waits for them, and re-layouts: 13.4 us -> 17.5 us
  matrix products: 19.4 us -> 16 us
    all_gather x1, blocking collectives: 28.7 us -> 82.9 us  [on_device(): lax.all_gather(norm_weights, 'shard', axis=1, tiled=True)]
    all_gather x1 -> x0, waiting for transfers between devices: 49 us -> none  [on_device(): lax.all_gather(owned_down, 'shard', axis=0, tiled=True)]
    all_gather x1, waiting for transfers between devices: 49 us -> 27.9 us  [on_device(): lax.all_gather(owned_up, 'shard', axis=0, tiled=True)]
    all_to_all x0 -> x1, starting transfers between devices: none -> 11.7 us  [_solve_cube(): lax.all_to_all(jnp.stack([m for _ in range(lax.axis_size('shard'))]), 'sh...]
    all_gather x1, waiting for transfers between devices: 8.47 us -> 0.01 us  [on_device(): lax.all_gather(owned_sq, 'shard', axis=1, tiled=True)]
    another operation x0 -> x1, local copies, waits for them, and re-layouts: none -> 2.72 us  [_solve_cube(): jnp.stack([m for _ in range(lax.axis_size('shard'))])]
    unnamed x30 -> x34, local copies, waits for them, and re-layouts: 12.8 us -> 14.2 us
  transfers between devices with their start and end apart: 3 -> 3, of which waited for: 3 -> 1; matrix products, arithmetic and copies ran while one was open for 7% -> 8% of each run, Pallas kernels for 0% -> 0%
where the time goes in v1:
time: 190 us; the launch traced here: 189 us
  blocking collectives  99.7 us (52%)
  waiting for transfers between devices  28 us (15%)
  local copies, waits for them, and re-layouts  17.5 us (9%)
  matrix products  16 us (8%)
  between operations  14.2 us (7%)
  starting transfers between devices  11.8 us (6%)
  other arithmetic  2.14 us (1%)
    all_gather x1, blocking collectives, on_device(): lax.all_gather(norm_weights, 'shard', axis=1, tiled=True)  82.9 us
    all_gather x1, waiting for transfers between devices, on_device(): lax.all_gather(owned_up, 'shard', axis=0, tiled=True)  27.9 us
    psum x1, blocking collectives, on_device(): summed = lax.psum((factor_sq, factor_up, factor_down, norm_delta), 'rep')  16.8 us
    unnamed x34, local copies, waits for them, and re-layouts  14.2 us
    all_to_all x1, starting transfers between devices, _solve_cube(): lax.all_to_all(jnp.stack([m for _ in range(lax.axis_size('shard'))]), 'sh...  11.7 us
  transfers between devices with their start and end apart: 3, of which 1 were waited for; matrix products, arithmetic and copies ran while one was open for 8% of the time, Pallas kernels for 0%

profile of v1, /device:TPU:1, one launch (start us, length us, event | category | flops | bytes accessed | tf_op | source)
XLA Modules:
  0.0 189.4 jit_solution(17082023390325959224)
XLA Ops:
  7.2 0.0 copy-start
  7.2 0.0 copy-start.5
  7.2 0.0 copy-start.4
  7.2 0.0 copy-start.6
  7.2 0.0 copy-start.3
  7.2 0.0 copy-start.1
  7.3 0.0 copy-start.11
  7.3 0.0 copy-start.12
  7.3 0.0 all-gather.4.cloned.1.call-start
  7.3 0.9 bitcast_subtract_fusion.3
  8.2 0.6 copy-done
  8.8 1.9 %fusion.16 = f32[4,24,64]{2,1,0:T(8,128)S(1)} fusion(f32[4,768,64]{1,2,0:T(8,128)S(1)} %copy-done, f32[1,4,24,768]{3,2,1,0:T(8,128)} %param.26, f32[4,24,768]{2,1,0:T(8,128)} %param.22, f32[1,4,24,768]{3,2,1,0:T(8,128)} %param.18), kind=kOutput, calls=%fused_computation.34 | convolution fusion | flops 56770560 | bytes 1695744 | tf_op jit(solution)/shard_map/mrd,mdk->mrk/dot_general | solution.py:51
  10.7 0.0 copy-start.10
  10.7 1.6 fusion.18
  12.3 0.0 copy-start.13
  12.4 2.1 %fusion.17 = f32[24,64]{1,0:T(8,128)S(1)} fusion(f32[3072,64]{0,1:T(8,128)} %param.34, f32[1,24,3072]{2,1,0:T(8,128)} %param.27, f32[24,3072]{1,0:T(8,128)} %param.23, f32[1,24,3072]{2,1,0:T(8,128)} %param.19), kind=kOutput, calls=%fused_computation.35 | convolution fusion | flops 56770560 | bytes 1677312 | tf_op jit(solution)/shard_map/dot_general | solution.py:54
  14.5 16.8 %all-reduce = (f32[4,24,64]{2,1,0:T(8,128)S(1)}, f32[24,64]{1,0:T(8,128)S(1)}, f32[96,64]{0,1:T(8,128)S(1)}, f32[4,24]{1,0:T(4,128)}) all-reduce(f32[4,24,64]{2,1,0:T(8,128)S(1)} %fusion.16, f32[24,64]{1,0:T(8,128)S(1)} %fusion.17, f32[96,64]{0,1:T(8,128)S(1)} %fusion.18, ...), channel_id=1, replica_groups=mesh['rep'=4,'shard'=32] {'rep'}, use_global_device_ids=true, to_apply=%region_0.0 | all-reduce | flops 13920 | bytes 111360 | tf_op jit(solution)/shard_map/psum | solution.py:64
  31.3 0.0 copy-done.5
  31.3 0.0 copy-done.11
  31.3 1.3 subtract_convert_fusion.2
  32.6 0.0 all-gather.4.cloned.1.call-update
  32.6 0.0 all-gather.6.cloned.1.call-start
  32.7 0.0 copy-done.3
  32.7 0.0 copy-done.1
  32.7 0.0 copy-done.12
  32.7 1.3 subtract_convert_fusion.1
  34.0 0.0 all-gather.6.cloned.1.call-update
  34.0 0.0 copy-done.4
  34.1 0.0 copy-done.6
  34.1 2.2 %subtract_convert_fusion = (bf16[96,768]{1,0:T(8,128)(2,1)S(1)}, f32[96,768]{1,0:T(8,128)}) fusion(f32[96,768]{1,0:T(8,128)S(1)} %copy-done.4, f32[96,768]{1,0:T(8,128)} %param.31, f32[768,64]{0,1:T(8,128)S(1)} %copy-done.6, f32[96,64]{0,1:T(8,128)S(1)} %get-tuple-element.13), kind=kOutput, calls=%fused_computation.12 | convolution fusion | flops 57145344 | bytes 1253376 | tf_op jit(solution)/shard_map/rk,dk->rd/dot_general | solution.py:72
  36.2 0.0 copy-done.10
  36.2 0.0 copy-done.13
  36.2 2.7 %stack.2 = bf16[32,96,768]{2,1,0:T(8,128)(2,1)} broadcast(bf16[96,768]{1,0:T(8,128)(2,1)S(1)} %get-tuple-element.17), dimensions={1,2} | broadcast | bytes 4866048 | tf_op jit(solution)/shard_map/stack | solution.py:13
  39.0 11.7 %all-to-all-start = ((bf16[32,96,768]{2,1,0:T(8,128)(2,1)}), bf16[32,96,768]{2,1,0:T(8,128)(2,1)}, u32[]{:S(2)}, u32[]{:S(2)}) async-start(bf16[32,96,768]{2,1,0:T(8,128)(2,1)} %stack.2), calls=%async_computation | async-start | bytes 9437184 | tf_op jit(solution)/shard_map/all_to_all | solution.py:13
  50.7 0.0 copy-done.14
  50.7 1.3 fusion.12
  52.0 82.9 %all-gather = bf16[32,24,4]{1,2,0:T(4,128)(2,1)S(1)} all-gather(bf16[1,24,4]{1,2,0:T(4,128)(2,1)S(1)} %get-tuple-element.15), channel_id=1, replica_groups=mesh['rep'=4,'shard'=32] {'shard'}, dimensions={0}, use_global_device_ids=true | all-gather | bytes 6336 | tf_op jit(solution)/shard_map/all_gather | solution.py:80
  134.9 0.6 copy.30
  135.5 1.5 reshape.29
  137.0 0.0 copy-done.9
  137.0 2.1 %fusion.1 = f32[1,96,768]{2,1,0:T(8,128)} fusion(f32[96,64]{0,1:T(8,128)} %copy-done.13, f32[768,64]{0,1:T(8,128)S(1)} %copy-done.6, f32[1,96,768]{2,1,0:T(8,128)S(1)} %copy-done.9, f32[96,768]{1,0:T(8,128)S(1)} %copy-done.4, f32[1,96,768]{2,1,0:T(8,128)} %param.20), kind=kOutput, calls=%fused_computation.3 | convolution fusion | flops 56844288 | bytes 1400832 | tf_op jit(solution)/shard_map/rk,dk->rd/dot_general | solution.py:60
  139.1 1.2 fusion
  140.3 2.3 %fusion.2 = f32[1,4,24,768]{3,2,1,0:T(8,128)} fusion(f32[4,24,64]{2,1,0:T(8,128)} %copy-done.10, f32[4,768,64]{1,2,0:T(8,128)S(1)} %copy-done, f32[1,4,24,768]{3,2,1,0:T(8,128)} %param.26, f32[4,24,768]{2,1,0:T(8,128)S(1)} %copy-done.5, f32[1,4,24,768]{3,2,1,0:T(8,128)} %param.18), kind=kOutput, calls=%fused_computation.5 | convolution fusion | flops 56844288 | bytes 1990656 | tf_op jit(solution)/shard_map/mrk,mdk->mrd/dot_general | solution.py:52
  142.6 0.0 all-to-all-done
  142.6 27.9 %all-gather.6.cloned.1.call-done = bf16[768,3072]{1,0:T(8,128)(2,1)} async-done(((bf16[24,3072]{1,0:T(8,128)(2,1)}), bf16[768,3072]{1,0:T(8,128)(2,1)}) %all-gather.6.cloned.1.call-update) | async-done | bytes 4718608 | tf_op jit(solution)/shard_map/all_gather | solution.py:78
  170.6 5.0 %copy.34 = bf16[4,768,768]{2,1,0:T(8,128)(2,1)} copy(bf16[4,768,768]{2,1,0:T(8,128)(2,1)} %all-gather.4.cloned.1.call-done) | data formatting | bytes 9437184
  175.6 2.2 %copy.35 = bf16[768,3072]{1,0:T(8,128)(2,1)} copy(bf16[768,3072]{1,0:T(8,128)(2,1)S(1)} %copy-done.2) | data formatting | bytes 9437184
  177.8 4.8 %copy.36 = bf16[3072,768]{1,0:T(8,128)(2,1)} copy(bf16[3072,768]{1,0:T(8,128)(2,1)} %bitcast.10) | data formatting | bytes 9437184
  (9 shorter events, 0.0 us)
Async XLA Ops:
  7.2 1.6 copy-start
  7.2 24.1 %copy-start.5 = (f32[4,24,768]{2,1,0:T(8,128)S(1)}, f32[4,24,768]{2,1,0:T(8,128)}, u32[]{:S(2)}) copy-start(f32[4,24,768]{2,1,0:T(8,128)} %param.22) | copy-start | bytes 884740
  7.2 26.8 %copy-start.4 = (f32[96,768]{1,0:T(8,128)S(1)}, f32[96,768]{1,0:T(8,128)}, u32[]{:S(2)}) copy-start(f32[96,768]{1,0:T(8,128)} %param.24) | copy-start | bytes 884740
  7.2 26.8 %copy-start.6 = (f32[768,64]{0,1:T(8,128)S(1)}, f32[768,64]{0,1:T(8,128)}, u32[]{:S(2)}) copy-start(f32[768,64]{0,1:T(8,128)} %param.35) | copy-start | bytes 589828
  7.2 25.5 %copy-start.3 = (f32[24,3072]{1,0:T(8,128)S(1)}, f32[24,3072]{1,0:T(8,128)}, u32[]{:S(2)}) copy-start(f32[24,3072]{1,0:T(8,128)} %param.23) | copy-start | bytes 884740
  7.2 25.5 %copy-start.1 = (f32[3072,64]{0,1:T(8,128)S(1)}, f32[3072,64]{0,1:T(8,128)}, u32[]{:S(2)}) copy-start(f32[3072,64]{0,1:T(8,128)} %param.34) | copy-start | bytes 2359300
  7.3 24.1 %copy-start.11 = (f32[4,24,768]{2,1,0:T(8,128)S(1)}, f32[4,24,768]{2,1,0:T(8,128)}, u32[]{:S(2)}) copy-start(f32[4,24,768]{2,1,0:T(8,128)} %param.29) | copy-start | bytes 884740
  7.3 25.4 %copy-start.12 = (f32[24,3072]{1,0:T(8,128)S(1)}, f32[24,3072]{1,0:T(8,128)}, u32[]{:S(2)}) copy-start(f32[24,3072]{1,0:T(8,128)} %param.30) | copy-start | bytes 884740
  7.3 135.4 %all-gather.4.cloned.1.call-start = ((), (), s32[]{:S(2)}) async-start(), calls=%async_computation.1 | async-start | bytes 4866048 | tf_op jit(solution)/shard_map/all_gather | solution.py:77
  10.7 25.5 %copy-start.10 = (f32[4,24,64]{2,1,0:T(8,128)}, f32[4,24,64]{2,1,0:T(8,128)S(1)}, u32[]{:S(2)}) copy-start(f32[4,24,64]{2,1,0:T(8,128)S(1)} %fusion.16) | copy-start | bytes 73732
  12.3 23.9 %copy-start.13 = (f32[96,64]{0,1:T(8,128)}, f32[96,64]{0,1:T(8,128)S(1)}, u32[]{:S(2)}) copy-start(f32[96,64]{0,1:T(8,128)S(1)} %fusion.18) | copy-start | bytes 73732
  32.6 137.9 %all-gather.6.cloned.1.call-start = ((), (), s32[]{:S(2)}) async-start(), calls=%async_computation.2 | async-start | bytes 4866048 | tf_op jit(solution)/shard_map/all_gather | solution.py:78
  39.0 11.7 %copy-start.14 = (f32[4,24]{1,0:T(4,128)S(1)}, f32[4,24]{1,0:T(4,128)}, u32[]{:S(2)}) copy-start(f32[4,24]{1,0:T(4,128)} %param.25) | copy-start | bytes 1156
  39.0 98.0 %copy-start.9 = (f32[1,96,768]{2,1,0:T(8,128)S(1)}, f32[1,96,768]{2,1,0:T(8,128)}, u32[]{:S(2)}) copy-start(f32[1,96,768]{2,1,0:T(8,128)} %param.28) | copy-start | bytes 884740
  39.0 100.2 %copy-start.7 = (f32[1,24,3072]{2,1,0:T(8,128)S(1)}, f32[1,24,3072]{2,1,0:T(8,128)}, u32[]{:S(2)}) copy-start(f32[1,24,3072]{2,1,0:T(8,128)} %param.27) | copy-start | bytes 884740
  39.0 100.2 %copy-start.8 = (f32[1,24,3072]{2,1,0:T(8,128)S(1)}, f32[1,24,3072]{2,1,0:T(8,128)}, u32[]{:S(2)}) copy-start(f32[1,24,3072]{2,1,0:T(8,128)} %param.19) | copy-start | bytes 884740
  39.0 103.7 %all-to-all-start = ((bf16[32,96,768]{2,1,0:T(8,128)(2,1)}), bf16[32,96,768]{2,1,0:T(8,128)(2,1)}, u32[]{:S(2)}, u32[]{:S(2)}) async-start(bf16[32,96,768]{2,1,0:T(8,128)(2,1)} %stack.2), calls=%async_computation | async-start | bytes 9437184 | tf_op jit(solution)/shard_map/all_to_all | solution.py:13
  170.6 5.0 %copy-start.2 = (bf16[768,3072]{1,0:T(8,128)(2,1)S(1)}, bf16[768,3072]{1,0:T(8,128)(2,1)}, u32[]{:S(2)}) copy-start(bf16[768,3072]{1,0:T(8,128)(2,1)} %all-gather.6.cloned.1.call-done) | copy-start | bytes 14155780
Sparse Core Ops, SparseCore 0:
  32.8 88.9 all-gather.3
  124.6 45.9 all-gather.5
